TPU v7x, 256 devices: a whole 4x4x8 slice. The times are simulated.
256 devices in a mesh: layer: 32 (over z, y), plane: 8 (over x, core).
Axes of the slice: x: 4, y: 4, z: 8, core: 2. Of those that a mesh axis runs over, the one named last changes fastest.
Arguments:
- rhs_field: float32 [32, 2, 4, 64, 1024], P('layer', None, None, None, 'plane'), may hold values from -6 to 6
- panel_inverse: bfloat16 [32, 1024, 2048], P('layer'), may hold values from -1 to 1
- coupling: float32 [32, 2, 4, 64], P('layer', None, None, 'plane'), may hold values from -0.98 to 0.98, as said below
Outputs:
- sweep_field: float32 [32, 2, 4, 64, 1024], P('layer', None, None, None, 'plane')
Inputs may be any that keep to these rules, and one draw needn't show every extreme that they name: Every complex coupling has modulus at most 0.98.
All inputs are finite; a program needn't handle non-finite values.
Results may differ from a plain program's by a relative error of at most 0.025.
Values may be sent and summed in bfloat16 or wider, within the bound.
No kernel may reach another device: no remote copies, remote signals or barrier semaphores. Data moves between devices by JAX's collectives and lax.ppermute only.
A program may use at most 64 MiB of HBM per device.

v0:
```python
import jax
import jax.numpy as jnp
from jax import lax
from jax.experimental import pallas as pl
from jax.experimental.pallas import tpu as pltpu
from jax.sharding import PartitionSpec as P


def kernel_mix(source, factor, carried):
    real = source[0] + (factor[0] * carried[0] - factor[1] * carried[1])
    imag = source[1] + (factor[0] * carried[1] + factor[1] * carried[0])
    return real.astype(jnp.bfloat16), imag.astype(jnp.bfloat16)


def kernel_twist(factor, field):
    real = factor[0] * field[0] - factor[1] * field[1]
    imag = factor[0] * field[1] + factor[1] * field[0]
    return real.astype(jnp.bfloat16), imag.astype(jnp.bfloat16)


def product_into(rows, inverse, out, base=None):
    count = rows[0].shape[0]
    width = inverse.shape[0]
    part = 256
    flat = jnp.concatenate(rows, axis=0)

    def chunk(index, carry):
        low = pl.multiple_of(index * part, part)
        high = pl.multiple_of(width + index * part, part)
        left = jnp.dot(flat, inverse[:, pl.ds(low, part)], preferred_element_type=jnp.float32)
        right = jnp.dot(flat, inverse[:, pl.ds(high, part)], preferred_element_type=jnp.float32)
        real = left[:count] - right[count:]
        imag = right[:count] + left[count:]
        if base is not None:
            real = base[0, :, pl.ds(low, part)] + real
            imag = base[1, :, pl.ds(low, part)] + imag
        out[0, :, pl.ds(low, part)] = real
        out[1, :, pl.ds(low, part)] = imag
        return carry

    lax.fori_loop(0, width // part, chunk, 0)
    return read(out)


def read(ref):
    return ref[0], ref[1]


def write(ref, pair):
    ref[0] = pair[0]
    ref[1] = pair[1]


def widen(pair):
    return tuple(part.astype(jnp.bfloat16).astype(jnp.float32) for part in pair)


def forward_kernel(single, *refs):
    if single:
        incoming, source, factor, inverse, first_out, outgoing, held, sems = refs
    else:
        (incoming, source, factor, source_next, factor_next, inverse, inverse_next,
         first_out, second_out, outgoing, held, sems) = refs
    copies = [pltpu.make_async_copy(inverse, held.at[0], sems.at[0])]
    if not single:
        copies.append(pltpu.make_async_copy(inverse_next, held.at[1], sems.at[1]))
    for copy in copies:
        copy.start()
    carried = tuple(part.astype(jnp.float32) for part in read(incoming))
    mixed = kernel_mix(read(source), read(factor), carried)
    copies[0].wait()
    first = product_into(mixed, held.at[0], first_out)
    if single:
        write(outgoing, tuple(part.astype(jnp.bfloat16) for part in first))
        return
    mixed = kernel_mix(read(source_next), read(factor_next), widen(first))
    copies[1].wait()
    second = product_into(mixed, held.at[1], second_out)
    write(outgoing, tuple(part.astype(jnp.bfloat16) for part in second))


def quad_forward_kernel(incoming, *refs):
    sources, factors, inverses = refs[0:4], refs[4:8], refs[8:12]
    stores, held, sems = refs[12:16], refs[16], refs[17]
    copies = [pltpu.make_async_copy(inverses[i], held.at[i], sems.at[i]) for i in range(4)]
    for panel in range(2):
        copies[panel].start()
    carried = tuple(part.astype(jnp.float32) for part in read(incoming))
    for panel in range(4):
        mixed = kernel_mix(read(sources[panel]), read(factors[panel]), carried)
        copies[panel].wait()
        if panel + 2 < 4:
            copies[panel + 2].start()
        result = product_into(mixed, held.at[panel], stores[panel])
        carried = widen(result)


def quad_forward_call(args, shape, width):
    local = pl.BlockSpec(memory_space=pltpu.VMEM)
    remote = pl.BlockSpec(memory_space=pl.ANY)
    rows = 2 * shape[0] * shape[1]
    return pl.pallas_call(
        quad_forward_kernel,
        out_shape=tuple([jax.ShapeDtypeStruct(shape, jnp.float32)] * 4),
        in_specs=[local] * 9 + [remote] * 4,
        out_specs=tuple([local] * 4),
        scratch_shapes=[pltpu.VMEM((4, width, 2 * width), jnp.bfloat16),
                        pltpu.SemaphoreType.DMA((4,))],
        compiler_params=pltpu.CompilerParams(vmem_limit_bytes=56 * 1024 * 1024),
        cost_estimate=pl.CostEstimate(
            flops=4 * 2 * rows * width * 2 * width, transcendentals=0,
            bytes_accessed=4 * width * 2 * width * 2 + 13 * rows * width * 4),
    )(*args)


def quad_kernel(skip, incoming, *refs):
    stores, factors, inverses = refs[0:4], refs[4:8], refs[8:12]
    sweeps, outgoing, held, sems = refs[12:16], refs[16], refs[17], refs[18]
    order = [2, 1, 0] if skip else [3, 2, 1, 0]
    copies = {i: pltpu.make_async_copy(inverses[i], held.at[i], sems.at[i]) for i in order}
    for panel in order[:2]:
        copies[panel].start()
    queued = 2
    carried = read(incoming)
    for panel in (3, 2, 1, 0):
        if skip and panel == 3:
            sweep = read(stores[panel])
            write(sweeps[panel], sweep)
        else:
            copies[panel].wait()
            if queued < len(order):
                copies[order[queued]].start()
                queued += 1
            sweep = product_into(carried, held.at[panel], sweeps[panel], stores[panel])
        carried = kernel_twist(read(factors[panel]), sweep)
    write(outgoing, carried)


def quad_call(skip, args, shape, width):
    local = pl.BlockSpec(memory_space=pltpu.VMEM)
    remote = pl.BlockSpec(memory_space=pl.ANY)
    rows = 2 * shape[0] * shape[1]
    matmuls = 3 if skip else 4
    out_shape = [jax.ShapeDtypeStruct(shape, jnp.float32)] * 4
    out_shape.append(jax.ShapeDtypeStruct(shape, jnp.bfloat16))
    return pl.pallas_call(
        lambda *refs: quad_kernel(skip, *refs),
        out_shape=tuple(out_shape),
        in_specs=[local] * 9 + [remote] * 4,
        out_specs=tuple([local] * 5),
        scratch_shapes=[pltpu.VMEM((4, width, 2 * width), jnp.bfloat16),
                        pltpu.SemaphoreType.DMA((4,))],
        compiler_params=pltpu.CompilerParams(vmem_limit_bytes=56 * 1024 * 1024),
        cost_estimate=pl.CostEstimate(
            flops=matmuls * 2 * rows * width * 2 * width, transcendentals=0,
            bytes_accessed=matmuls * width * 2 * width * 2 + 14 * rows * width * 4),
    )(*args)


def pair_call(kernel, args, shape, width, matmuls, remotes, results):
    local = pl.BlockSpec(memory_space=pltpu.VMEM)
    remote = pl.BlockSpec(memory_space=pl.ANY)
    rows = 2 * shape[0] * shape[1]
    out_shape = [jax.ShapeDtypeStruct(shape, jnp.float32)] * (results - 1)
    out_shape.append(jax.ShapeDtypeStruct(shape, jnp.bfloat16))
    return pl.pallas_call(
        kernel,
        out_shape=tuple(out_shape),
        in_specs=[local] * (len(args) - remotes) + [remote] * remotes,
        out_specs=tuple([local] * results),
        scratch_shapes=[pltpu.VMEM((2, width, 2 * width), jnp.bfloat16),
                        pltpu.SemaphoreType.DMA((2,))],
        compiler_params=pltpu.CompilerParams(vmem_limit_bytes=48 * 1024 * 1024),
        cost_estimate=pl.CostEstimate(
            flops=matmuls * 2 * rows * width * 2 * width, transcendentals=0,
            bytes_accessed=matmuls * width * 2 * width * 2 + 8 * rows * width * 4),
    )(*args)


def body(rhs_field, panel_inverse, coupling):
    planes = lax.axis_size("plane")
    layers = lax.axis_size("layer")
    place = lax.axis_index("layer")
    plane = lax.axis_index("plane")
    pairs = layers // 2

    block = rhs_field[0]
    parts, loads, ys, chunk = block.shape
    block = block.reshape(parts, loads, planes, ys // planes, chunk)
    block = jnp.moveaxis(block, 2, 0)
    block = lax.all_to_all(block, "plane", split_axis=0, concat_axis=0, tiled=True)
    lines = jnp.moveaxis(block, 0, 3).reshape(parts, loads * ys // planes, planes * chunk)
    shape = lines.shape

    inverse = panel_inverse[0]
    width = inverse.shape[0]
    factors = jnp.broadcast_to(coupling[0].reshape(parts, shape[1], 1), shape)
    down = [(2 * j + 1, 2 * j) for j in range(pairs)]

    rows = width // planes
    piece = lax.dynamic_slice_in_dim(inverse, plane * rows, rows, 0)
    own_piece = piece
    piece = lax.ppermute(piece, "layer", down)
    inverse_next = lax.all_gather(piece, "plane", axis=0, tiled=True)
    lines_next = lax.ppermute(lines, "layer", down)
    factors_next = lax.ppermute(factors, "layer", down)
    quads = layers // 4
    gather = [(4 * j + 2, 4 * j) for j in range(quads)]
    quad_factors = [lax.ppermute(factor, "layer", gather) for factor in (factors, factors_next)]
    last = layers - 4
    quad_lines = [lax.ppermute(source, "layer", [(last + 2, last)]) for source in (lines, lines_next)]

    zero = jnp.zeros(shape, jnp.float32)
    outgoing = jnp.zeros(shape, jnp.bfloat16)
    store_a, store_b = zero, zero
    for panel in range(2):
        if panel > 0:
            incoming = lax.ppermute(outgoing, "layer", [(panel - 1, panel)])
        else:
            incoming = outgoing

        def active(incoming, store_a, outgoing):
            kernel = lambda *refs: forward_kernel(True, *refs)
            return pair_call(kernel, (incoming, lines, factors, inverse), shape, width, 1, 1, 2)

        def idle(incoming, store_a, outgoing):
            return store_a, outgoing

        store_a, outgoing = lax.cond(place == panel, active, idle, incoming, store_a, outgoing)
    store_b = lax.ppermute(store_a, "layer", [(1, 0)])

    for section in range(1, pairs - 2):
        source = 1 if section == 1 else 2 * section - 2
        incoming = lax.ppermute(outgoing, "layer", [(source, 2 * section)])

        def active(incoming, store_a, store_b, outgoing):
            kernel = lambda *refs: forward_kernel(False, *refs)
            args = (incoming, lines, factors, lines_next, factors_next, inverse, inverse_next)
            return pair_call(kernel, args, shape, width, 2, 2, 3)

        def idle(incoming, store_a, store_b, outgoing):
            return store_a, store_b, outgoing

        store_a, store_b, outgoing = lax.cond(
            place == 2 * section, active, idle, incoming, store_a, store_b, outgoing)
        if section == min(7, pairs - 1):
            outgoing, moved = lax.optimization_barrier((outgoing, own_piece))
            quad_inverses = [
                lax.all_gather(lax.ppermute(moved, "layer", [(4 * j + offset, 4 * j) for j in range(quads)]),
                               "plane", axis=0, tiled=True)
                for offset in (2, 3)]

    incoming = lax.ppermute(outgoing, "layer", [(last - 2, last)])

    def active(incoming, store_a, store_b, extra_a, extra_b):
        args = ((incoming, lines, lines_next) + tuple(quad_lines) + (factors, factors_next)
                + tuple(quad_factors) + (inverse, inverse_next) + tuple(quad_inverses))
        return quad_forward_call(args, shape, width)

    def idle(incoming, store_a, store_b, extra_a, extra_b):
        return store_a, store_b, extra_a, extra_b

    store_a, store_b, extra_a, extra_b = lax.cond(
        place == last, active, idle, incoming, store_a, store_b, zero, zero)
    outgoing = jnp.zeros(shape, jnp.bfloat16)
    gather_stores = [(4 * j + 2, 4 * j) for j in range(quads - 1)]
    quad_stores = [jnp.where(place == last, extra, lax.ppermute(store, "layer", gather_stores))
                   for extra, store in ((extra_a, store_a), (extra_b, store_b))]

    sweeps = (zero, zero, zero, zero)
    for section in range(quads):
        lead = layers - 4 - 4 * section
        if section > 0:
            incoming = lax.ppermute(outgoing, "layer", [(lead + 4, lead)])
        else:
            incoming = outgoing

        def active(incoming, sweeps, outgoing, skip=(section == 0)):
            args = ((incoming, store_a, store_b) + tuple(quad_stores) + (factors, factors_next)
                    + tuple(quad_factors) + (inverse, inverse_next) + tuple(quad_inverses))
            results = quad_call(skip, args, shape, width)
            return tuple(results[:4]), results[4]

        def idle(incoming, sweeps, outgoing):
            return sweeps, outgoing

        sweeps, outgoing = lax.cond(place == lead, active, idle, incoming, sweeps, outgoing)

    result = sweeps[0]
    for offset in (1, 2, 3):
        returned = lax.ppermute(sweeps[offset], "layer", [(4 * j, 4 * j + offset) for j in range(quads)])
        result = jnp.where(place % 4 == offset, returned, result)

    result = result.reshape(parts, loads, ys // planes, planes, chunk)
    result = jnp.moveaxis(result, 3, 0)
    result = lax.all_to_all(result, "plane", split_axis=0, concat_axis=0, tiled=True)
    result = jnp.moveaxis(result, 0, 2).reshape(parts, loads, ys, chunk)
    return result[None]


def solution(mesh):
    in_specs = (
        P("layer", None, None, None, "plane"),
        P("layer", None, None),
        P("layer", None, None, "plane"),
    )
    out_specs = P("layer", None, None, None, "plane")
    return jax.shard_map(body, mesh=mesh, in_specs=in_specs, out_specs=out_specs, check_vma=False)
```

profile of v0, /device:TPU:8, one launch (start us, length us, event | category | flops | bytes accessed | tf_op | source)
XLA Modules:
  0.0 355.3 jit_solution(14240477423504098185)
XLA Ops:
  6.5 1.1 dynamic-slice_bitcast_fusion
  7.6 4.1 %collective-permute-start.5 = (bf16[128,2048]{1,0:T(8,128)(2,1)S(1)}, bf16[128,2048]{1,0:T(8,128)(2,1)S(1)}, u32[]{:S(2)}, u32[]{:S(2)}) collective-permute-start(bf16[128,2048]{1,0:T(8,128)(2,1)S(1)} %dynamic-slice_bitcast_fusion), channel_id=1, source_target_pairs={{8,0},{24,16},{40,32},{56,48},{72,64},{88,80},{104,96},{120,112},{... | collective-permute-start | bytes 1572872 | tf_op jit(solution)/shard_map/ppermute | solution.py:203
  11.7 8.6 %collective-permute-done.5 = bf16[128,2048]{1,0:T(8,128)(2,1)S(1)} collective-permute-done((bf16[128,2048]{1,0:T(8,128)(2,1)S(1)}, bf16[128,2048]{1,0:T(8,128)(2,1)S(1)}, u32[]{:S(2)}, u32[]{:S(2)}) %collective-permute-start.5) | collective-permute-done | bytes 524320 | tf_op jit(solution)/shard_map/ppermute | solution.py:203
  20.4 0.8 copy-done.2
  21.2 1.7 copy.4
  22.8 5.1 %all-to-all-start = ((f32[8,2,4,8,128]{4,3,2,1,0:T(8,128)}), f32[8,2,4,8,128]{4,3,2,1,0:T(8,128)S(1)}, u32[]{:S(2)}, u32[]{:S(2)}) async-start(f32[8,2,4,8,128]{4,3,2,1,0:T(8,128)} %copy.4), calls=%async_computation | async-start | bytes 524288 | tf_op jit(solution)/shard_map/all_to_all | solution.py:191
  28.0 0.8 broadcast_in_dim.16
  28.7 6.7 %all-to-all-done = f32[8,2,4,8,128]{4,3,2,1,0:T(8,128)S(1)} async-done(((f32[8,2,4,8,128]{4,3,2,1,0:T(8,128)}), f32[8,2,4,8,128]{4,3,2,1,0:T(8,128)S(1)}, u32[]{:S(2)}, u32[]{:S(2)}) %all-to-all-start) | async-done | bytes 262176 | tf_op jit(solution)/shard_map/all_to_all | solution.py:191
  35.8 1.3 collective-permute-start
  37.1 9.2 %collective-permute-done = bf16[2,32,1024]{2,1,0:T(8,128)(2,1)S(1)} collective-permute-done((bf16[2,32,1024]{2,1,0:T(8,128)(2,1)S(1)}, bf16[2,32,1024]{2,1,0:T(8,128)(2,1)S(1)}, u32[]{:S(2)}, u32[]{:S(2)}) %collective-permute-start) | collective-permute-done | bytes 131104 | tf_op jit(solution)/shard_map/ppermute | solution.py:218
  46.3 3.5 conditional.25
  46.3 3.5 branch_1_fun.25
  49.9 1.3 collective-permute-start.1
  51.2 1.3 collective-permute-start.4
  52.5 1.3 collective-permute-start.3
  53.8 1.3 collective-permute-start.2
  55.1 2.7 collective-permute-done.1
  57.9 5.6 %collective-permute-done.4 = f32[2,32,1024]{2,1,0:T(8,128)S(1)} collective-permute-done((f32[2,32,1024]{2,1,0:T(8,128)S(1)}, f32[2,32,1024]{2,1,0:T(8,128)S(1)}, u32[]{:S(2)}, u32[]{:S(2)}) %collective-permute-start.4) | collective-permute-done | bytes 262176 | tf_op jit(solution)/shard_map/ppermute | solution.py:206
  63.5 3.9 %collective-permute-done.3 = f32[2,32,1024]{2,1,0:T(8,128)S(1)} collective-permute-done((f32[2,32,1024]{2,1,0:T(8,128)S(1)}, f32[2,32,1024]{2,1,0:T(8,128)S(1)}, u32[]{:S(2)}, u32[]{:S(2)}) %collective-permute-start.3) | collective-permute-done | bytes 262176 | tf_op jit(solution)/shard_map/ppermute | solution.py:205
  71.6 0.7 collective-permute-start.23
  72.3 0.8 copy-done
  73.2 0.7 collective-permute-start.24
  73.9 0.8 copy-done.1
  78.9 0.7 collective-permute-start.21
  79.6 0.7 collective-permute-start.19
  82.4 92.1 %all-gather.6.cloned.1.call-done = bf16[1024,2048]{1,0:T(8,128)(2,1)} async-done(((bf16[128,2048]{1,0:T(8,128)(2,1)}), bf16[1024,2048]{1,0:T(8,128)(2,1)}) %all-gather.6.cloned.1.call-update) | async-done | bytes 4194320 | tf_op jit(solution)/shard_map/all_gather | solution.py:249
  174.5 36.5 %all-gather.8.cloned.1.call-done = bf16[1024,2048]{1,0:T(8,128)(2,1)} async-done(((bf16[128,2048]{1,0:T(8,128)(2,1)}), bf16[1024,2048]{1,0:T(8,128)(2,1)}) %all-gather.8.cloned.1.call-update) | async-done | bytes 4194320 | tf_op jit(solution)/shard_map/all_gather | solution.py:249
  211.7 0.9 collective-permute-start.25
  219.2 1.3 collective-permute-start.36
  220.5 117.4 %collective-permute-done.36 = f32[2,32,1024]{2,1,0:T(8,128)S(1)} collective-permute-done((f32[2,32,1024]{2,1,0:T(8,128)S(1)}, f32[2,32,1024]{2,1,0:T(8,128)S(1)}, u32[]{:S(2)}, u32[]{:S(2)}) %collective-permute-start.36) | collective-permute-done | bytes 262176 | tf_op jit(solution)/shard_map/ppermute | solution.py:291
  338.0 10.1 %all_to_all.10 = f32[8,2,4,8,128]{4,3,2,1,0:T(8,128)S(1)} all-to-all(f32[8,2,4,8,128]{4,3,2,1,0:T(8,128)S(1)} %copy.6), channel_id=1, replica_groups=mesh['layer'=32,'plane'=8] {'plane'}, dimensions={0} | all-to-all | bytes 524288 | tf_op jit(solution)/shard_map/all_to_all | solution.py:296
  348.1 0.7 copy.11
  (105 shorter events, 18.0 us)
Async XLA Ops:
  6.5 60.8 %all-gather.4.cloned.1.call-start = ((), (), s32[]{:S(2)}) async-start(), calls=%async_computation.2 | async-start | bytes 4718592 | tf_op jit(solution)/shard_map/all_gather | solution.py:204
  7.6 12.7 %collective-permute-start.5 = (bf16[128,2048]{1,0:T(8,128)(2,1)S(1)}, bf16[128,2048]{1,0:T(8,128)(2,1)S(1)}, u32[]{:S(2)}, u32[]{:S(2)}) collective-permute-start(bf16[128,2048]{1,0:T(8,128)(2,1)S(1)} %dynamic-slice_bitcast_fusion), channel_id=1, source_target_pairs={{8,0},{24,16},{40,32},{56,48},{72,64},{88,80},{104,96},{120,112},{... | collective-permute-start | bytes 1572872 | tf_op jit(solution)/shard_map/ppermute | solution.py:203
  22.8 12.6 %all-to-all-start = ((f32[8,2,4,8,128]{4,3,2,1,0:T(8,128)}), f32[8,2,4,8,128]{4,3,2,1,0:T(8,128)S(1)}, u32[]{:S(2)}, u32[]{:S(2)}) async-start(f32[8,2,4,8,128]{4,3,2,1,0:T(8,128)} %copy.4), calls=%async_computation | async-start | bytes 524288 | tf_op jit(solution)/shard_map/all_to_all | solution.py:191
  27.9 146.6 %all-gather.6.cloned.1.call-start = ((), (), s32[]{:S(2)}) async-start(), calls=%async_computation.3 | async-start | bytes 4718592 | tf_op jit(solution)/shard_map/all_gather | solution.py:249
  35.8 10.5 %collective-permute-start = (bf16[2,32,1024]{2,1,0:T(8,128)(2,1)S(1)}, bf16[2,32,1024]{2,1,0:T(8,128)(2,1)S(1)}, u32[]{:S(2)}, u32[]{:S(2)}) collective-permute-start(bf16[2,32,1024]{2,1,0:T(8,128)(2,1)S(1)} %get-tuple-element.848), channel_id=1, source_target_pairs={{0,8},{1,9},{2,10},{3,11},{4,12},{5,13},{6,14},{7,15}} | collective-permute-start | bytes 393224 | tf_op jit(solution)/shard_map/ppermute | solution.py:218
  49.9 8.0 %collective-permute-start.1 = (f32[2,32,1024]{2,1,0:T(8,128)S(1)}, f32[2,32,1024]{2,1,0:T(8,128)S(1)}, u32[]{:S(2)}, u32[]{:S(2)}) collective-permute-start(f32[2,32,1024]{2,1,0:T(8,128)S(1)} %get-tuple-element.849), channel_id=1, source_target_pairs={{8,0},{9,1},{10,2},{11,3},{12,4},{13,5},{14,6},{15,7}} | collective-permute-start | bytes 786440 | tf_op jit(solution)/shard_map/ppermute | solution.py:230
  51.2 12.3 %collective-permute-start.4 = (f32[2,32,1024]{2,1,0:T(8,128)S(1)}, f32[2,32,1024]{2,1,0:T(8,128)S(1)}, u32[]{:S(2)}, u32[]{:S(2)}) collective-permute-start(f32[2,32,1024]{2,1,0:T(8,128)S(1)} %broadcast_in_dim.17), channel_id=1, source_target_pairs={{8,0},{24,16},{40,32},{56,48},{72,64},{88,80},{104,96},{120,112},{... | collective-permute-start | bytes 786440 | tf_op jit(solution)/shard_map/ppermute | solution.py:206
  52.5 14.9 %collective-permute-start.3 = (f32[2,32,1024]{2,1,0:T(8,128)S(1)}, f32[2,32,1024]{2,1,0:T(8,128)S(1)}, u32[]{:S(2)}, u32[]{:S(2)}) collective-permute-start(f32[2,32,1024]{2,1,0:T(8,128)S(1)} %reshape.8), channel_id=1, source_target_pairs={{8,0},{24,16},{40,32},{56,48},{72,64},{88,80},{104,96},{120,112},{... | collective-permute-start | bytes 786440 | tf_op jit(solution)/shard_map/ppermute | solution.py:205
  53.8 9.7 %collective-permute-start.2 = (bf16[2,32,1024]{2,1,0:T(8,128)(2,1)S(1)}, bf16[2,32,1024]{2,1,0:T(8,128)(2,1)S(1)}, u32[]{:S(2)}, u32[]{:S(2)}) collective-permute-start(bf16[2,32,1024]{2,1,0:T(8,128)(2,1)S(1)} %get-tuple-element.850), channel_id=1, source_target_pairs={{8,16},{9,17},{10,18},{11,19},{12,20},{13,21},{14,22},{15,23}} | collective-permute-start | bytes 393224 | tf_op jit(solution)/shard_map/ppermute | solution.py:234
  68.1 0.7 collective-permute-start.7
  68.8 0.7 collective-permute-start.8
  70.2 0.7 collective-permute-start.10
  70.9 0.7 collective-permute-start.11
  71.6 0.7 collective-permute-start.23
  73.1 137.9 %all-gather.8.cloned.1.call-start = ((), (), s32[]{:S(2)}) async-start(), calls=%async_computation.4 | async-start | bytes 4718592 | tf_op jit(solution)/shard_map/all_gather | solution.py:249
  73.2 0.7 collective-permute-start.24
  74.7 0.7 collective-permute-start.12
  75.4 0.7 collective-permute-start.13
  76.1 0.7 collective-permute-start.14
  76.8 0.7 collective-permute-start.15
  77.6 0.7 collective-permute-start.16
  78.3 3.4 collective-permute-start.17
  78.9 3.5 collective-permute-start.21
  79.6 2.8 collective-permute-start.19
  80.3 2.1 collective-permute-start.22
  81.0 1.4 collective-permute-start.20
  81.7 0.7 collective-permute-start.18
  211.1 1.6 collective-permute-start.26
  211.7 0.9 collective-permute-start.25
  217.8 2.7 collective-permute-start.34
  218.5 2.0 collective-permute-start.35
  219.2 118.7 %collective-permute-start.36 = (f32[2,32,1024]{2,1,0:T(8,128)S(1)}, f32[2,32,1024]{2,1,0:T(8,128)S(1)}, u32[]{:S(2)}, u32[]{:S(2)}) collective-permute-start(f32[2,32,1024]{2,1,0:T(8,128)S(1)} %get-tuple-element.887), channel_id=1, source_target_pairs={{0,8},{32,40},{64,72},{96,104},{128,136},{160,168},{192,200},{224,... | collective-permute-start | bytes 786440 | tf_op jit(solution)/shard_map/ppermute | solution.py:291
  (12 other events, 8.5 us)
Sparse Core Ops, SparseCore 0:
  21.3 40.2 all-gather.3
  73.3 101.2 all-gather.5
  176.4 34.5 all-gather.7
where the time goes:
time: 356 us; the launch traced here: 355 us
  waiting for transfers between devices  283 us (79%)
  starting transfers between devices  37.4 us (11%)
  between operations  14 us (4%)
  blocking collectives  10.1 us (3%)
  local copies, waits for them, and re-layouts  7.06 us (2%)
    all_gather x2, waiting for transfers between devices, body(): lax.all_gather(lax.ppermute(moved, 'layer', [(4 * j + offset, 4 * j) for...  129 us
    ppermute x3, waiting for transfers between devices, body(): lax.ppermute(sweeps[offset], 'layer', [(4 * j, 4 * j + offset) for j in r...  117 us
    all_to_all x1, blocking collectives, body(): lax.all_to_all(result, 'plane', split_axis=0, concat_axis=0, tiled=True)  10.1 us
    ppermute x13, starting transfers between devices, body(): incoming = lax.ppermute(outgoing, 'layer', [(source, 2 * section)])  9.31 us
    ppermute x1, waiting for transfers between devices, body(): incoming = lax.ppermute(outgoing, 'layer', [(panel - 1, panel)])  9.24 us
    ppermute x1, waiting for transfers between devices, body(): piece = lax.ppermute(piece, 'layer', down)  8.64 us
  transfers between devices with their start and end apart: 41, of which 9 were waited for; matrix products, arithmetic and copies ran while one was open for 1% of the time, Pallas kernels for 1%

commit v1 on v0

--- a/solution.py
+++ b/solution.py
@@ -21,7 +21,7 @@
 def product_into(rows, inverse, out, base=None):
     count = rows[0].shape[0]
     width = inverse.shape[0]
-    part = 256
+    part = 512
     flat = jnp.concatenate(rows, axis=0)
 
     def chunk(index, carry):

time: 356 us -> 349 us (0.980)
  waiting for transfers between devices: 283 us -> 277 us
    ppermute x3, waiting for transfers between devices: 117 us -> 113 us  [body(): lax.ppermute(sweeps[offset], 'layer', [(4 * j, 4 * j + offset) for j in r...]
where the time goes in v1:
time: 349 us
  waiting for transfers between devices  277 us (79%)
  starting transfers between devices  37.2 us (11%)
  between operations  14 us (4%)
  blocking collectives  9.94 us (3%)
  local copies, waits for them, and re-layouts  7.06 us (2%)
    all_gather x2, waiting for transfers between devices, body(): lax.all_gather(lax.ppermute(moved, 'layer', [(4 * j + offset, 4 * j) for...  127 us
    ppermute x3, waiting for transfers between devices, body(): lax.ppermute(sweeps[offset], 'layer', [(4 * j, 4 * j + offset) for j in r...  113 us
    all_to_all x1, blocking collectives, body(): lax.all_to_all(result, 'plane', split_axis=0, concat_axis=0, tiled=True)  9.94 us
    ppermute x13, starting transfers between devices, body(): incoming = lax.ppermute(outgoing, 'layer', [(source, 2 * section)])  9.31 us
    ppermute x1, waiting for transfers between devices, body(): incoming = lax.ppermute(outgoing, 'layer', [(panel - 1, panel)])  9 us
    ppermute x1, waiting for transfers between devices, body(): piece = lax.ppermute(piece, 'layer', down)  8.64 us
  transfers between devices with their start and end apart: 41, of which 9 were waited for; matrix products, arithmetic and copies ran while one was open for 1% of the time, Pallas kernels for 1%

profile of v1, /device:TPU:8, one launch (start us, length us, event | category | flops | bytes accessed | tf_op | source)
XLA Modules:
  0.0 348.5 jit_solution(10975865329459057346)
XLA Ops:
  6.5 1.1 dynamic-slice_bitcast_fusion
  7.6 4.1 %collective-permute-start.5 = (bf16[128,2048]{1,0:T(8,128)(2,1)S(1)}, bf16[128,2048]{1,0:T(8,128)(2,1)S(1)}, u32[]{:S(2)}, u32[]{:S(2)}) collective-permute-start(bf16[128,2048]{1,0:T(8,128)(2,1)S(1)} %dynamic-slice_bitcast_fusion), channel_id=1, source_target_pairs={{8,0},{24,16},{40,32},{56,48},{72,64},{88,80},{104,96},{120,112},{... | collective-permute-start | bytes 1572872 | tf_op jit(solution)/shard_map/ppermute | solution.py:203
  11.7 8.6 %collective-permute-done.5 = bf16[128,2048]{1,0:T(8,128)(2,1)S(1)} collective-permute-done((bf16[128,2048]{1,0:T(8,128)(2,1)S(1)}, bf16[128,2048]{1,0:T(8,128)(2,1)S(1)}, u32[]{:S(2)}, u32[]{:S(2)}) %collective-permute-start.5) | collective-permute-done | bytes 524320 | tf_op jit(solution)/shard_map/ppermute | solution.py:203
  20.4 0.8 copy-done.2
  21.2 1.7 copy.4
  22.8 5.1 %all-to-all-start = ((f32[8,2,4,8,128]{4,3,2,1,0:T(8,128)}), f32[8,2,4,8,128]{4,3,2,1,0:T(8,128)S(1)}, u32[]{:S(2)}, u32[]{:S(2)}) async-start(f32[8,2,4,8,128]{4,3,2,1,0:T(8,128)} %copy.4), calls=%async_computation | async-start | bytes 524288 | tf_op jit(solution)/shard_map/all_to_all | solution.py:191
  28.0 0.8 broadcast_in_dim.16
  28.7 6.7 %all-to-all-done = f32[8,2,4,8,128]{4,3,2,1,0:T(8,128)S(1)} async-done(((f32[8,2,4,8,128]{4,3,2,1,0:T(8,128)}), f32[8,2,4,8,128]{4,3,2,1,0:T(8,128)S(1)}, u32[]{:S(2)}, u32[]{:S(2)}) %all-to-all-start) | async-done | bytes 262176 | tf_op jit(solution)/shard_map/all_to_all | solution.py:191
  35.8 1.3 collective-permute-start
  37.1 9.0 %collective-permute-done = bf16[2,32,1024]{2,1,0:T(8,128)(2,1)S(1)} collective-permute-done((bf16[2,32,1024]{2,1,0:T(8,128)(2,1)S(1)}, bf16[2,32,1024]{2,1,0:T(8,128)(2,1)S(1)}, u32[]{:S(2)}, u32[]{:S(2)}) %collective-permute-start) | collective-permute-done | bytes 131104 | tf_op jit(solution)/shard_map/ppermute | solution.py:218
  46.1 3.3 conditional.25
  46.1 3.3 branch_1_fun.25
  49.4 1.3 collective-permute-start.1
  50.7 1.3 collective-permute-start.4
  52.0 1.3 collective-permute-start.3
  53.3 1.3 collective-permute-start.2
  54.6 2.7 collective-permute-done.1
  57.4 5.6 %collective-permute-done.4 = f32[2,32,1024]{2,1,0:T(8,128)S(1)} collective-permute-done((f32[2,32,1024]{2,1,0:T(8,128)S(1)}, f32[2,32,1024]{2,1,0:T(8,128)S(1)}, u32[]{:S(2)}, u32[]{:S(2)}) %collective-permute-start.4) | collective-permute-done | bytes 262176 | tf_op jit(solution)/shard_map/ppermute | solution.py:206
  63.0 3.9 %collective-permute-done.3 = f32[2,32,1024]{2,1,0:T(8,128)S(1)} collective-permute-done((f32[2,32,1024]{2,1,0:T(8,128)S(1)}, f32[2,32,1024]{2,1,0:T(8,128)S(1)}, u32[]{:S(2)}, u32[]{:S(2)}) %collective-permute-start.3) | collective-permute-done | bytes 262176 | tf_op jit(solution)/shard_map/ppermute | solution.py:205
  71.1 0.7 collective-permute-start.23
  71.8 0.8 copy-done
  72.7 0.7 collective-permute-start.24
  73.4 0.8 copy-done.1
  78.4 0.7 collective-permute-start.21
  79.1 0.7 collective-permute-start.19
  79.8 0.7 collective-permute-start.22
  82.1 90.5 %all-gather.6.cloned.1.call-done = bf16[1024,2048]{1,0:T(8,128)(2,1)} async-done(((bf16[128,2048]{1,0:T(8,128)(2,1)}), bf16[1024,2048]{1,0:T(8,128)(2,1)}) %all-gather.6.cloned.1.call-update) | async-done | bytes 4194320 | tf_op jit(solution)/shard_map/all_gather | solution.py:249
  172.7 36.5 %all-gather.8.cloned.1.call-done = bf16[1024,2048]{1,0:T(8,128)(2,1)} async-done(((bf16[128,2048]{1,0:T(8,128)(2,1)}), bf16[1024,2048]{1,0:T(8,128)(2,1)}) %all-gather.8.cloned.1.call-update) | async-done | bytes 4194320 | tf_op jit(solution)/shard_map/all_gather | solution.py:249
  217.1 1.3 collective-permute-start.36
  218.5 112.8 %collective-permute-done.36 = f32[2,32,1024]{2,1,0:T(8,128)S(1)} collective-permute-done((f32[2,32,1024]{2,1,0:T(8,128)S(1)}, f32[2,32,1024]{2,1,0:T(8,128)S(1)}, u32[]{:S(2)}, u32[]{:S(2)}) %collective-permute-start.36) | collective-permute-done | bytes 262176 | tf_op jit(solution)/shard_map/ppermute | solution.py:291
  331.3 9.9 %all_to_all.10 = f32[8,2,4,8,128]{4,3,2,1,0:T(8,128)S(1)} all-to-all(f32[8,2,4,8,128]{4,3,2,1,0:T(8,128)S(1)} %copy.6), channel_id=1, replica_groups=mesh['layer'=32,'plane'=8] {'plane'}, dimensions={0} | all-to-all | bytes 524288 | tf_op jit(solution)/shard_map/all_to_all | solution.py:296
  341.3 0.7 copy.11
  (105 shorter events, 18.1 us)
Async XLA Ops:
  6.5 60.4 %all-gather.4.cloned.1.call-start = ((), (), s32[]{:S(2)}) async-start(), calls=%async_computation.2 | async-start | bytes 4718592 | tf_op jit(solution)/shard_map/all_gather | solution.py:204
  7.6 12.7 %collective-permute-start.5 = (bf16[128,2048]{1,0:T(8,128)(2,1)S(1)}, bf16[128,2048]{1,0:T(8,128)(2,1)S(1)}, u32[]{:S(2)}, u32[]{:S(2)}) collective-permute-start(bf16[128,2048]{1,0:T(8,128)(2,1)S(1)} %dynamic-slice_bitcast_fusion), channel_id=1, source_target_pairs={{8,0},{24,16},{40,32},{56,48},{72,64},{88,80},{104,96},{120,112},{... | collective-permute-start | bytes 1572872 | tf_op jit(solution)/shard_map/ppermute | solution.py:203
  22.8 12.6 %all-to-all-start = ((f32[8,2,4,8,128]{4,3,2,1,0:T(8,128)}), f32[8,2,4,8,128]{4,3,2,1,0:T(8,128)S(1)}, u32[]{:S(2)}, u32[]{:S(2)}) async-start(f32[8,2,4,8,128]{4,3,2,1,0:T(8,128)} %copy.4), calls=%async_computation | async-start | bytes 524288 | tf_op jit(solution)/shard_map/all_to_all | solution.py:191
  27.9 144.7 %all-gather.6.cloned.1.call-start = ((), (), s32[]{:S(2)}) async-start(), calls=%async_computation.3 | async-start | bytes 4718592 | tf_op jit(solution)/shard_map/all_gather | solution.py:249
  35.8 10.3 %collective-permute-start = (bf16[2,32,1024]{2,1,0:T(8,128)(2,1)S(1)}, bf16[2,32,1024]{2,1,0:T(8,128)(2,1)S(1)}, u32[]{:S(2)}, u32[]{:S(2)}) collective-permute-start(bf16[2,32,1024]{2,1,0:T(8,128)(2,1)S(1)} %get-tuple-element.848), channel_id=1, source_target_pairs={{0,8},{1,9},{2,10},{3,11},{4,12},{5,13},{6,14},{7,15}} | collective-permute-start | bytes 393224 | tf_op jit(solution)/shard_map/ppermute | solution.py:218
  49.4 8.0 %collective-permute-start.1 = (f32[2,32,1024]{2,1,0:T(8,128)S(1)}, f32[2,32,1024]{2,1,0:T(8,128)S(1)}, u32[]{:S(2)}, u32[]{:S(2)}) collective-permute-start(f32[2,32,1024]{2,1,0:T(8,128)S(1)} %get-tuple-element.849), channel_id=1, source_target_pairs={{8,0},{9,1},{10,2},{11,3},{12,4},{13,5},{14,6},{15,7}} | collective-permute-start | bytes 786440 | tf_op jit(solution)/shard_map/ppermute | solution.py:230
  50.7 12.3 %collective-permute-start.4 = (f32[2,32,1024]{2,1,0:T(8,128)S(1)}, f32[2,32,1024]{2,1,0:T(8,128)S(1)}, u32[]{:S(2)}, u32[]{:S(2)}) collective-permute-start(f32[2,32,1024]{2,1,0:T(8,128)S(1)} %broadcast_in_dim.17), channel_id=1, source_target_pairs={{8,0},{24,16},{40,32},{56,48},{72,64},{88,80},{104,96},{120,112},{... | collective-permute-start | bytes 786440 | tf_op jit(solution)/shard_map/ppermute | solution.py:206
  52.0 14.9 %collective-permute-start.3 = (f32[2,32,1024]{2,1,0:T(8,128)S(1)}, f32[2,32,1024]{2,1,0:T(8,128)S(1)}, u32[]{:S(2)}, u32[]{:S(2)}) collective-permute-start(f32[2,32,1024]{2,1,0:T(8,128)S(1)} %reshape.8), channel_id=1, source_target_pairs={{8,0},{24,16},{40,32},{56,48},{72,64},{88,80},{104,96},{120,112},{... | collective-permute-start | bytes 786440 | tf_op jit(solution)/shard_map/ppermute | solution.py:205
  53.3 9.7 %collective-permute-start.2 = (bf16[2,32,1024]{2,1,0:T(8,128)(2,1)S(1)}, bf16[2,32,1024]{2,1,0:T(8,128)(2,1)S(1)}, u32[]{:S(2)}, u32[]{:S(2)}) collective-permute-start(bf16[2,32,1024]{2,1,0:T(8,128)(2,1)S(1)} %get-tuple-element.850), channel_id=1, source_target_pairs={{8,16},{9,17},{10,18},{11,19},{12,20},{13,21},{14,22},{15,23}} | collective-permute-start | bytes 393224 | tf_op jit(solution)/shard_map/ppermute | solution.py:234
  67.6 0.7 collective-permute-start.7
  68.3 0.7 collective-permute-start.8
  69.7 0.7 collective-permute-start.10
  70.4 0.7 collective-permute-start.11
  71.1 0.7 collective-permute-start.23
  72.6 136.5 %all-gather.8.cloned.1.call-start = ((), (), s32[]{:S(2)}) async-start(), calls=%async_computation.4 | async-start | bytes 4718592 | tf_op jit(solution)/shard_map/all_gather | solution.py:249
  72.7 0.7 collective-permute-start.24
  74.2 0.7 collective-permute-start.12
  74.9 0.7 collective-permute-start.13
  75.7 0.7 collective-permute-start.14
  76.4 0.7 collective-permute-start.15
  77.1 0.7 collective-permute-start.16
  77.8 3.4 collective-permute-start.17
  78.4 3.6 %collective-permute-start.21 = (f32[2,32,1024]{2,1,0:T(8,128)S(1)}, f32[2,32,1024]{2,1,0:T(8,128)S(1)}, u32[]{:S(2)}, u32[]{:S(2)}) collective-permute-start(f32[2,32,1024]{2,1,0:T(8,128)S(1)} %broadcast_in_dim.17), channel_id=1, source_target_pairs={{16,0},{48,32},{80,64},{112,96},{144,128},{176,160},{208,192},{240... | collective-permute-start | bytes 786440 | tf_op jit(solution)/shard_map/ppermute | solution.py:209
  79.1 3.0 collective-permute-start.19
  79.8 2.3 collective-permute-start.22
  80.5 1.6 collective-permute-start.20
  81.4 0.7 collective-permute-start.18
  209.2 1.4 collective-permute-start.26
  209.9 0.7 collective-permute-start.25
  215.8 2.7 collective-permute-start.34
  216.4 2.0 collective-permute-start.35
  217.1 114.1 %collective-permute-start.36 = (f32[2,32,1024]{2,1,0:T(8,128)S(1)}, f32[2,32,1024]{2,1,0:T(8,128)S(1)}, u32[]{:S(2)}, u32[]{:S(2)}) collective-permute-start(f32[2,32,1024]{2,1,0:T(8,128)S(1)} %get-tuple-element.887), channel_id=1, source_target_pairs={{0,8},{32,40},{64,72},{96,104},{128,136},{160,168},{192,200},{224,... | collective-permute-start | bytes 786440 | tf_op jit(solution)/shard_map/ppermute | solution.py:291
  (12 other events, 8.5 us)
Sparse Core Ops, SparseCore 0:
  21.3 40.2 all-gather.3
  72.8 99.8 all-gather.5
  174.5 34.5 all-gather.7

commit v2 on v1

--- a/solution.py
+++ b/solution.py
@@ -83,14 +83,14 @@
     sources, factors, inverses = refs[0:4], refs[4:8], refs[8:12]
     stores, held, sems = refs[12:16], refs[16], refs[17]
     copies = [pltpu.make_async_copy(inverses[i], held.at[i], sems.at[i]) for i in range(4)]
-    for panel in range(2):
+    for panel in range(3):
         copies[panel].start()
     carried = tuple(part.astype(jnp.float32) for part in read(incoming))
     for panel in range(4):
         mixed = kernel_mix(read(sources[panel]), read(factors[panel]), carried)
         copies[panel].wait()
-        if panel + 2 < 4:
-            copies[panel + 2].start()
+        if panel + 3 < 4:
+            copies[panel + 3].start()
         result = product_into(mixed, held.at[panel], stores[panel])
         carried = widen(result)
 
@@ -118,9 +118,9 @@
     sweeps, outgoing, held, sems = refs[12:16], refs[16], refs[17], refs[18]
     order = [2, 1, 0] if skip else [3, 2, 1, 0]
     copies = {i: pltpu.make_async_copy(inverses[i], held.at[i], sems.at[i]) for i in order}
-    for panel in order[:2]:
+    for panel in order[:3]:
         copies[panel].start()
-    queued = 2
+    queued = 3
     carried = read(incoming)
     for panel in (3, 2, 1, 0):
         if skip and panel == 3:

time: 349 us -> 349 us (level)
  no operation moved by 1% of the time
where the time goes in v2:
time: 349 us
  waiting for transfers between devices  277 us (79%)
  starting transfers between devices  37.2 us (11%)
  between operations  14 us (4%)
  blocking collectives  9.94 us (3%)
  local copies, waits for them, and re-layouts  7.06 us (2%)
    all_gather x2, waiting for transfers between devices, body(): lax.all_gather(lax.ppermute(moved, 'layer', [(4 * j + offset, 4 * j) for...  127 us
    ppermute x3, waiting for transfers between devices, body(): lax.ppermute(sweeps[offset], 'layer', [(4 * j, 4 * j + offset) for j in r...  113 us
    all_to_all x1, blocking collectives, body(): lax.all_to_all(result, 'plane', split_axis=0, concat_axis=0, tiled=True)  9.94 us
    ppermute x13, starting transfers between devices, body(): incoming = lax.ppermute(outgoing, 'layer', [(source, 2 * section)])  9.31 us
    ppermute x1, waiting for transfers between devices, body(): incoming = lax.ppermute(outgoing, 'layer', [(panel - 1, panel)])  9 us
    ppermute x1, waiting for transfers between devices, body(): piece = lax.ppermute(piece, 'layer', down)  8.64 us
  transfers between devices with their start and end apart: 41, of which 9 were waited for; matrix products, arithmetic and copies ran while one was open for 1% of the time, Pallas kernels for 1%

profile of v2, /device:TPU:8, one launch (start us, length us, event | category | flops | bytes accessed | tf_op | source)
XLA Modules:
  0.0 348.6 jit_solution(14918872608195693043)
XLA Ops:
  6.5 1.1 dynamic-slice_bitcast_fusion
  7.6 4.1 %collective-permute-start.5 = (bf16[128,2048]{1,0:T(8,128)(2,1)S(1)}, bf16[128,2048]{1,0:T(8,128)(2,1)S(1)}, u32[]{:S(2)}, u32[]{:S(2)}) collective-permute-start(bf16[128,2048]{1,0:T(8,128)(2,1)S(1)} %dynamic-slice_bitcast_fusion), channel_id=1, source_target_pairs={{8,0},{24,16},{40,32},{56,48},{72,64},{88,80},{104,96},{120,112},{... | collective-permute-start | bytes 1572872 | tf_op jit(solution)/shard_map/ppermute | solution.py:203
  11.7 8.6 %collective-permute-done.5 = bf16[128,2048]{1,0:T(8,128)(2,1)S(1)} collective-permute-done((bf16[128,2048]{1,0:T(8,128)(2,1)S(1)}, bf16[128,2048]{1,0:T(8,128)(2,1)S(1)}, u32[]{:S(2)}, u32[]{:S(2)}) %collective-permute-start.5) | collective-permute-done | bytes 524320 | tf_op jit(solution)/shard_map/ppermute | solution.py:203
  20.4 0.8 copy-done.2
  21.2 1.7 copy.4
  22.8 5.1 %all-to-all-start = ((f32[8,2,4,8,128]{4,3,2,1,0:T(8,128)}), f32[8,2,4,8,128]{4,3,2,1,0:T(8,128)S(1)}, u32[]{:S(2)}, u32[]{:S(2)}) async-start(f32[8,2,4,8,128]{4,3,2,1,0:T(8,128)} %copy.4), calls=%async_computation | async-start | bytes 524288 | tf_op jit(solution)/shard_map/all_to_all | solution.py:191
  28.0 0.8 broadcast_in_dim.16
  28.7 6.7 %all-to-all-done = f32[8,2,4,8,128]{4,3,2,1,0:T(8,128)S(1)} async-done(((f32[8,2,4,8,128]{4,3,2,1,0:T(8,128)}), f32[8,2,4,8,128]{4,3,2,1,0:T(8,128)S(1)}, u32[]{:S(2)}, u32[]{:S(2)}) %all-to-all-start) | async-done | bytes 262176 | tf_op jit(solution)/shard_map/all_to_all | solution.py:191
  35.8 1.3 collective-permute-start
  37.1 9.0 %collective-permute-done = bf16[2,32,1024]{2,1,0:T(8,128)(2,1)S(1)} collective-permute-done((bf16[2,32,1024]{2,1,0:T(8,128)(2,1)S(1)}, bf16[2,32,1024]{2,1,0:T(8,128)(2,1)S(1)}, u32[]{:S(2)}, u32[]{:S(2)}) %collective-permute-start) | collective-permute-done | bytes 131104 | tf_op jit(solution)/shard_map/ppermute | solution.py:218
  46.1 3.3 conditional.25
  46.1 3.3 branch_1_fun.25
  49.4 1.3 collective-permute-start.1
  50.7 1.3 collective-permute-start.4
  52.0 1.3 collective-permute-start.3
  53.3 1.3 collective-permute-start.2
  54.6 2.7 collective-permute-done.1
  57.4 5.6 %collective-permute-done.4 = f32[2,32,1024]{2,1,0:T(8,128)S(1)} collective-permute-done((f32[2,32,1024]{2,1,0:T(8,128)S(1)}, f32[2,32,1024]{2,1,0:T(8,128)S(1)}, u32[]{:S(2)}, u32[]{:S(2)}) %collective-permute-start.4) | collective-permute-done | bytes 262176 | tf_op jit(solution)/shard_map/ppermute | solution.py:206
  63.0 3.9 %collective-permute-done.3 = f32[2,32,1024]{2,1,0:T(8,128)S(1)} collective-permute-done((f32[2,32,1024]{2,1,0:T(8,128)S(1)}, f32[2,32,1024]{2,1,0:T(8,128)S(1)}, u32[]{:S(2)}, u32[]{:S(2)}) %collective-permute-start.3) | collective-permute-done | bytes 262176 | tf_op jit(solution)/shard_map/ppermute | solution.py:205
  71.1 0.7 collective-permute-start.23
  71.8 0.8 copy-done
  72.7 0.7 collective-permute-start.24
  73.4 0.8 copy-done.1
  78.4 0.7 collective-permute-start.21
  79.1 0.7 collective-permute-start.19
  79.8 0.7 collective-permute-start.22
  82.1 90.5 %all-gather.6.cloned.1.call-done = bf16[1024,2048]{1,0:T(8,128)(2,1)} async-done(((bf16[128,2048]{1,0:T(8,128)(2,1)}), bf16[1024,2048]{1,0:T(8,128)(2,1)}) %all-gather.6.cloned.1.call-update) | async-done | bytes 4194320 | tf_op jit(solution)/shard_map/all_gather | solution.py:249
  172.7 36.5 %all-gather.8.cloned.1.call-done = bf16[1024,2048]{1,0:T(8,128)(2,1)} async-done(((bf16[128,2048]{1,0:T(8,128)(2,1)}), bf16[1024,2048]{1,0:T(8,128)(2,1)}) %all-gather.8.cloned.1.call-update) | async-done | bytes 4194320 | tf_op jit(solution)/shard_map/all_gather | solution.py:249
  217.1 1.3 collective-permute-start.36
  218.5 112.8 %collective-permute-done.36 = f32[2,32,1024]{2,1,0:T(8,128)S(1)} collective-permute-done((f32[2,32,1024]{2,1,0:T(8,128)S(1)}, f32[2,32,1024]{2,1,0:T(8,128)S(1)}, u32[]{:S(2)}, u32[]{:S(2)}) %collective-permute-start.36) | collective-permute-done | bytes 262176 | tf_op jit(solution)/shard_map/ppermute | solution.py:291
  331.4 9.9 %all_to_all.10 = f32[8,2,4,8,128]{4,3,2,1,0:T(8,128)S(1)} all-to-all(f32[8,2,4,8,128]{4,3,2,1,0:T(8,128)S(1)} %copy.6), channel_id=1, replica_groups=mesh['layer'=32,'plane'=8] {'plane'}, dimensions={0} | all-to-all | bytes 524288 | tf_op jit(solution)/shard_map/all_to_all | solution.py:296
  341.3 0.7 copy.11
  (105 shorter events, 18.1 us)
Async XLA Ops:
  6.5 60.4 %all-gather.4.cloned.1.call-start = ((), (), s32[]{:S(2)}) async-start(), calls=%async_computation.2 | async-start | bytes 4718592 | tf_op jit(solution)/shard_map/all_gather | solution.py:204
  7.6 12.7 %collective-permute-start.5 = (bf16[128,2048]{1,0:T(8,128)(2,1)S(1)}, bf16[128,2048]{1,0:T(8,128)(2,1)S(1)}, u32[]{:S(2)}, u32[]{:S(2)}) collective-permute-start(bf16[128,2048]{1,0:T(8,128)(2,1)S(1)} %dynamic-slice_bitcast_fusion), channel_id=1, source_target_pairs={{8,0},{24,16},{40,32},{56,48},{72,64},{88,80},{104,96},{120,112},{... | collective-permute-start | bytes 1572872 | tf_op jit(solution)/shard_map/ppermute | solution.py:203
  22.8 12.6 %all-to-all-start = ((f32[8,2,4,8,128]{4,3,2,1,0:T(8,128)}), f32[8,2,4,8,128]{4,3,2,1,0:T(8,128)S(1)}, u32[]{:S(2)}, u32[]{:S(2)}) async-start(f32[8,2,4,8,128]{4,3,2,1,0:T(8,128)} %copy.4), calls=%async_computation | async-start | bytes 524288 | tf_op jit(solution)/shard_map/all_to_all | solution.py:191
  27.9 144.7 %all-gather.6.cloned.1.call-start = ((), (), s32[]{:S(2)}) async-start(), calls=%async_computation.3 | async-start | bytes 4718592 | tf_op jit(solution)/shard_map/all_gather | solution.py:249
  35.8 10.3 %collective-permute-start = (bf16[2,32,1024]{2,1,0:T(8,128)(2,1)S(1)}, bf16[2,32,1024]{2,1,0:T(8,128)(2,1)S(1)}, u32[]{:S(2)}, u32[]{:S(2)}) collective-permute-start(bf16[2,32,1024]{2,1,0:T(8,128)(2,1)S(1)} %get-tuple-element.848), channel_id=1, source_target_pairs={{0,8},{1,9},{2,10},{3,11},{4,12},{5,13},{6,14},{7,15}} | collective-permute-start | bytes 393224 | tf_op jit(solution)/shard_map/ppermute | solution.py:218
  49.4 8.0 %collective-permute-start.1 = (f32[2,32,1024]{2,1,0:T(8,128)S(1)}, f32[2,32,1024]{2,1,0:T(8,128)S(1)}, u32[]{:S(2)}, u32[]{:S(2)}) collective-permute-start(f32[2,32,1024]{2,1,0:T(8,128)S(1)} %get-tuple-element.849), channel_id=1, source_target_pairs={{8,0},{9,1},{10,2},{11,3},{12,4},{13,5},{14,6},{15,7}} | collective-permute-start | bytes 786440 | tf_op jit(solution)/shard_map/ppermute | solution.py:230
  50.7 12.3 %collective-permute-start.4 = (f32[2,32,1024]{2,1,0:T(8,128)S(1)}, f32[2,32,1024]{2,1,0:T(8,128)S(1)}, u32[]{:S(2)}, u32[]{:S(2)}) collective-permute-start(f32[2,32,1024]{2,1,0:T(8,128)S(1)} %broadcast_in_dim.17), channel_id=1, source_target_pairs={{8,0},{24,16},{40,32},{56,48},{72,64},{88,80},{104,96},{120,112},{... | collective-permute-start | bytes 786440 | tf_op jit(solution)/shard_map/ppermute | solution.py:206
  52.0 14.9 %collective-permute-start.3 = (f32[2,32,1024]{2,1,0:T(8,128)S(1)}, f32[2,32,1024]{2,1,0:T(8,128)S(1)}, u32[]{:S(2)}, u32[]{:S(2)}) collective-permute-start(f32[2,32,1024]{2,1,0:T(8,128)S(1)} %reshape.8), channel_id=1, source_target_pairs={{8,0},{24,16},{40,32},{56,48},{72,64},{88,80},{104,96},{120,112},{... | collective-permute-start | bytes 786440 | tf_op jit(solution)/shard_map/ppermute | solution.py:205
  53.3 9.7 %collective-permute-start.2 = (bf16[2,32,1024]{2,1,0:T(8,128)(2,1)S(1)}, bf16[2,32,1024]{2,1,0:T(8,128)(2,1)S(1)}, u32[]{:S(2)}, u32[]{:S(2)}) collective-permute-start(bf16[2,32,1024]{2,1,0:T(8,128)(2,1)S(1)} %get-tuple-element.850), channel_id=1, source_target_pairs={{8,16},{9,17},{10,18},{11,19},{12,20},{13,21},{14,22},{15,23}} | collective-permute-start | bytes 393224 | tf_op jit(solution)/shard_map/ppermute | solution.py:234
  67.6 0.7 collective-permute-start.7
  68.3 0.7 collective-permute-start.8
  69.7 0.7 collective-permute-start.10
  70.4 0.7 collective-permute-start.11
  71.1 0.7 collective-permute-start.23
  72.6 136.5 %all-gather.8.cloned.1.call-start = ((), (), s32[]{:S(2)}) async-start(), calls=%async_computation.4 | async-start | bytes 4718592 | tf_op jit(solution)/shard_map/all_gather | solution.py:249
  72.7 0.7 collective-permute-start.24
  74.2 0.7 collective-permute-start.12
  74.9 0.7 collective-permute-start.13
  75.7 0.7 collective-permute-start.14
  76.4 0.7 collective-permute-start.15
  77.1 0.7 collective-permute-start.16
  77.8 3.4 collective-permute-start.17
  78.4 3.6 %collective-permute-start.21 = (f32[2,32,1024]{2,1,0:T(8,128)S(1)}, f32[2,32,1024]{2,1,0:T(8,128)S(1)}, u32[]{:S(2)}, u32[]{:S(2)}) collective-permute-start(f32[2,32,1024]{2,1,0:T(8,128)S(1)} %broadcast_in_dim.17), channel_id=1, source_target_pairs={{16,0},{48,32},{80,64},{112,96},{144,128},{176,160},{208,192},{240... | collective-permute-start | bytes 786440 | tf_op jit(solution)/shard_map/ppermute | solution.py:209
  79.1 3.0 collective-permute-start.19
  79.8 2.3 collective-permute-start.22
  80.5 1.6 collective-permute-start.20
  81.4 0.7 collective-permute-start.18
  209.2 1.4 collective-permute-start.26
  209.9 0.7 collective-permute-start.25
  215.8 2.7 collective-permute-start.34
  216.4 2.0 collective-permute-start.35
  217.1 114.2 %collective-permute-start.36 = (f32[2,32,1024]{2,1,0:T(8,128)S(1)}, f32[2,32,1024]{2,1,0:T(8,128)S(1)}, u32[]{:S(2)}, u32[]{:S(2)}) collective-permute-start(f32[2,32,1024]{2,1,0:T(8,128)S(1)} %get-tuple-element.887), channel_id=1, source_target_pairs={{0,8},{32,40},{64,72},{96,104},{128,136},{160,168},{192,200},{224,... | collective-permute-start | bytes 786440 | tf_op jit(solution)/shard_map/ppermute | solution.py:291
  (12 other events, 8.5 us)
Sparse Core Ops, SparseCore 0:
  21.3 40.2 all-gather.3
  72.8 99.8 all-gather.5
  174.5 34.5 all-gather.7

commit v3 on v1

--- a/solution.py
+++ b/solution.py
@@ -55,26 +55,37 @@
     return tuple(part.astype(jnp.bfloat16).astype(jnp.float32) for part in pair)
 
 
+def half_copies(inverse, slot, sems):
+    width = inverse.shape[0]
+    return [pltpu.make_async_copy(inverse.at[:, pl.ds(half * width, width)],
+                                  slot.at[:, pl.ds(half * width, width)], sems.at[half])
+            for half in range(2)]
+
+
 def forward_kernel(single, *refs):
     if single:
         incoming, source, factor, inverse, first_out, outgoing, held, sems = refs
     else:
         (incoming, source, factor, source_next, factor_next, inverse, inverse_next,
          first_out, second_out, outgoing, held, sems) = refs
-    copies = [pltpu.make_async_copy(inverse, held.at[0], sems.at[0])]
-    if not single:
-        copies.append(pltpu.make_async_copy(inverse_next, held.at[1], sems.at[1]))
-    for copy in copies:
+    first_copies = half_copies(inverse, held.at[0], sems.at[0])
+    for copy in first_copies:
         copy.start()
     carried = tuple(part.astype(jnp.float32) for part in read(incoming))
     mixed = kernel_mix(read(source), read(factor), carried)
-    copies[0].wait()
+    for copy in first_copies:
+        copy.wait()
+    if not single:
+        second_copies = half_copies(inverse_next, held.at[1], sems.at[1])
+        for copy in second_copies:
+            copy.start()
     first = product_into(mixed, held.at[0], first_out)
     if single:
         write(outgoing, tuple(part.astype(jnp.bfloat16) for part in first))
         return
     mixed = kernel_mix(read(source_next), read(factor_next), widen(first))
-    copies[1].wait()
+    for copy in second_copies:
+        copy.wait()
     second = product_into(mixed, held.at[1], second_out)
     write(outgoing, tuple(part.astype(jnp.bfloat16) for part in second))
 
@@ -169,7 +180,7 @@
         in_specs=[local] * (len(args) - remotes) + [remote] * remotes,
         out_specs=tuple([local] * results),
         scratch_shapes=[pltpu.VMEM((2, width, 2 * width), jnp.bfloat16),
-                        pltpu.SemaphoreType.DMA((2,))],
+                        pltpu.SemaphoreType.DMA((2, 2))],
         compiler_params=pltpu.CompilerParams(vmem_limit_bytes=48 * 1024 * 1024),
         cost_estimate=pl.CostEstimate(
             flops=matmuls * 2 * rows * width * 2 * width, transcendentals=0,

time: 349 us -> 362 us (1.037)
  waiting for transfers between devices: 277 us -> 289 us
    all_gather x2, waiting for transfers between devices: 127 us -> 134 us  [body(): lax.all_gather(lax.ppermute(moved, 'layer', [(4 * j + offset, 4 * j) for...]
    ppermute x3, waiting for transfers between devices: 113 us -> 119 us  [body(): lax.ppermute(sweeps[offset], 'layer', [(4 * j, 4 * j + offset) for j in r...]
where the time goes in v3:
time: 362 us; the launch traced here: 361 us
  waiting for transfers between devices  289 us (80%)
  starting transfers between devices  37.2 us (10%)
  between operations  14 us (4%)
  blocking collectives  9.91 us (3%)
  local copies, waits for them, and re-layouts  7.06 us (2%)
    all_gather x2, waiting for transfers between devices, body(): lax.all_gather(lax.ppermute(moved, 'layer', [(4 * j + offset, 4 * j) for...  134 us
    ppermute x3, waiting for transfers between devices, body(): lax.ppermute(sweeps[offset], 'layer', [(4 * j, 4 * j + offset) for j in r...  119 us
    all_to_all x1, blocking collectives, body(): lax.all_to_all(result, 'plane', split_axis=0, concat_axis=0, tiled=True)  9.91 us
    ppermute x13, starting transfers between devices, body(): incoming = lax.ppermute(outgoing, 'layer', [(source, 2 * section)])  9.31 us
    ppermute x1, waiting for transfers between devices, body(): incoming = lax.ppermute(outgoing, 'layer', [(panel - 1, panel)])  9.04 us
    ppermute x1, waiting for transfers between devices, body(): piece = lax.ppermute(piece, 'layer', down)  8.64 us
  transfers between devices with their start and end apart: 41, of which 9 were waited for; matrix products, arithmetic and copies ran while one was open for 1% of the time, Pallas kernels for 1%

profile of v3, /device:TPU:8, one launch (start us, length us, event | category | flops | bytes accessed | tf_op | source)
XLA Modules:
  0.0 361.4 jit_solution(5023589203637475444)
XLA Ops:
  6.5 1.1 dynamic-slice_bitcast_fusion
  7.6 4.1 %collective-permute-start.5 = (bf16[128,2048]{1,0:T(8,128)(2,1)S(1)}, bf16[128,2048]{1,0:T(8,128)(2,1)S(1)}, u32[]{:S(2)}, u32[]{:S(2)}) collective-permute-start(bf16[128,2048]{1,0:T(8,128)(2,1)S(1)} %dynamic-slice_bitcast_fusion), channel_id=1, source_target_pairs={{8,0},{24,16},{40,32},{56,48},{72,64},{88,80},{104,96},{120,112},{... | collective-permute-start | bytes 1572872 | tf_op jit(solution)/shard_map/ppermute | solution.py:214
  11.7 8.6 %collective-permute-done.5 = bf16[128,2048]{1,0:T(8,128)(2,1)S(1)} collective-permute-done((bf16[128,2048]{1,0:T(8,128)(2,1)S(1)}, bf16[128,2048]{1,0:T(8,128)(2,1)S(1)}, u32[]{:S(2)}, u32[]{:S(2)}) %collective-permute-start.5) | collective-permute-done | bytes 524320 | tf_op jit(solution)/shard_map/ppermute | solution.py:214
  20.4 0.8 copy-done.2
  21.2 1.7 copy.4
  22.8 5.1 %all-to-all-start = ((f32[8,2,4,8,128]{4,3,2,1,0:T(8,128)}), f32[8,2,4,8,128]{4,3,2,1,0:T(8,128)S(1)}, u32[]{:S(2)}, u32[]{:S(2)}) async-start(f32[8,2,4,8,128]{4,3,2,1,0:T(8,128)} %copy.4), calls=%async_computation | async-start | bytes 524288 | tf_op jit(solution)/shard_map/all_to_all | solution.py:202
  28.0 0.8 broadcast_in_dim.16
  28.7 6.7 %all-to-all-done = f32[8,2,4,8,128]{4,3,2,1,0:T(8,128)S(1)} async-done(((f32[8,2,4,8,128]{4,3,2,1,0:T(8,128)}), f32[8,2,4,8,128]{4,3,2,1,0:T(8,128)S(1)}, u32[]{:S(2)}, u32[]{:S(2)}) %all-to-all-start) | async-done | bytes 262176 | tf_op jit(solution)/shard_map/all_to_all | solution.py:202
  35.8 1.3 collective-permute-start
  37.1 9.0 %collective-permute-done = bf16[2,32,1024]{2,1,0:T(8,128)(2,1)S(1)} collective-permute-done((bf16[2,32,1024]{2,1,0:T(8,128)(2,1)S(1)}, bf16[2,32,1024]{2,1,0:T(8,128)(2,1)S(1)}, u32[]{:S(2)}, u32[]{:S(2)}) %collective-permute-start) | collective-permute-done | bytes 131104 | tf_op jit(solution)/shard_map/ppermute | solution.py:229
  46.2 3.3 conditional.25
  46.2 3.3 branch_1_fun.25
  49.5 1.3 collective-permute-start.1
  50.8 1.3 collective-permute-start.4
  52.1 1.3 collective-permute-start.3
  53.4 1.3 collective-permute-start.2
  54.7 2.7 collective-permute-done.1
  57.5 5.6 %collective-permute-done.4 = f32[2,32,1024]{2,1,0:T(8,128)S(1)} collective-permute-done((f32[2,32,1024]{2,1,0:T(8,128)S(1)}, f32[2,32,1024]{2,1,0:T(8,128)S(1)}, u32[]{:S(2)}, u32[]{:S(2)}) %collective-permute-start.4) | collective-permute-done | bytes 262176 | tf_op jit(solution)/shard_map/ppermute | solution.py:217
  63.1 3.9 %collective-permute-done.3 = f32[2,32,1024]{2,1,0:T(8,128)S(1)} collective-permute-done((f32[2,32,1024]{2,1,0:T(8,128)S(1)}, f32[2,32,1024]{2,1,0:T(8,128)S(1)}, u32[]{:S(2)}, u32[]{:S(2)}) %collective-permute-start.3) | collective-permute-done | bytes 262176 | tf_op jit(solution)/shard_map/ppermute | solution.py:216
  71.2 0.7 collective-permute-start.23
  71.9 0.8 copy-done
  72.8 0.7 collective-permute-start.24
  73.5 0.8 copy-done.1
  78.5 0.7 collective-permute-start.21
  79.2 0.7 collective-permute-start.19
  82.1 97.6 %all-gather.6.cloned.1.call-done = bf16[1024,2048]{1,0:T(8,128)(2,1)} async-done(((bf16[128,2048]{1,0:T(8,128)(2,1)}), bf16[1024,2048]{1,0:T(8,128)(2,1)}) %all-gather.6.cloned.1.call-update) | async-done | bytes 4194320 | tf_op jit(solution)/shard_map/all_gather | solution.py:260
  179.6 36.5 %all-gather.8.cloned.1.call-done = bf16[1024,2048]{1,0:T(8,128)(2,1)} async-done(((bf16[128,2048]{1,0:T(8,128)(2,1)}), bf16[1024,2048]{1,0:T(8,128)(2,1)}) %all-gather.8.cloned.1.call-update) | async-done | bytes 4194320 | tf_op jit(solution)/shard_map/all_gather | solution.py:260
  216.3 0.7 collective-permute-start.26
  224.2 1.3 collective-permute-start.36
  225.6 118.6 %collective-permute-done.36 = f32[2,32,1024]{2,1,0:T(8,128)S(1)} collective-permute-done((f32[2,32,1024]{2,1,0:T(8,128)S(1)}, f32[2,32,1024]{2,1,0:T(8,128)S(1)}, u32[]{:S(2)}, u32[]{:S(2)}) %collective-permute-start.36) | collective-permute-done | bytes 262176 | tf_op jit(solution)/shard_map/ppermute | solution.py:302
  344.2 9.9 %all_to_all.10 = f32[8,2,4,8,128]{4,3,2,1,0:T(8,128)S(1)} all-to-all(f32[8,2,4,8,128]{4,3,2,1,0:T(8,128)S(1)} %copy.6), channel_id=1, replica_groups=mesh['layer'=32,'plane'=8] {'plane'}, dimensions={0} | all-to-all | bytes 524288 | tf_op jit(solution)/shard_map/all_to_all | solution.py:307
  354.1 0.7 copy.11
  (105 shorter events, 18.1 us)
Async XLA Ops:
  6.5 60.5 %all-gather.4.cloned.1.call-start = ((), (), s32[]{:S(2)}) async-start(), calls=%async_computation.2 | async-start | bytes 4718592 | tf_op jit(solution)/shard_map/all_gather | solution.py:215
  7.6 12.7 %collective-permute-start.5 = (bf16[128,2048]{1,0:T(8,128)(2,1)S(1)}, bf16[128,2048]{1,0:T(8,128)(2,1)S(1)}, u32[]{:S(2)}, u32[]{:S(2)}) collective-permute-start(bf16[128,2048]{1,0:T(8,128)(2,1)S(1)} %dynamic-slice_bitcast_fusion), channel_id=1, source_target_pairs={{8,0},{24,16},{40,32},{56,48},{72,64},{88,80},{104,96},{120,112},{... | collective-permute-start | bytes 1572872 | tf_op jit(solution)/shard_map/ppermute | solution.py:214
  22.8 12.6 %all-to-all-start = ((f32[8,2,4,8,128]{4,3,2,1,0:T(8,128)}), f32[8,2,4,8,128]{4,3,2,1,0:T(8,128)S(1)}, u32[]{:S(2)}, u32[]{:S(2)}) async-start(f32[8,2,4,8,128]{4,3,2,1,0:T(8,128)} %copy.4), calls=%async_computation | async-start | bytes 524288 | tf_op jit(solution)/shard_map/all_to_all | solution.py:202
  27.9 151.7 %all-gather.6.cloned.1.call-start = ((), (), s32[]{:S(2)}) async-start(), calls=%async_computation.3 | async-start | bytes 4718592 | tf_op jit(solution)/shard_map/all_gather | solution.py:260
  35.8 10.3 %collective-permute-start = (bf16[2,32,1024]{2,1,0:T(8,128)(2,1)S(1)}, bf16[2,32,1024]{2,1,0:T(8,128)(2,1)S(1)}, u32[]{:S(2)}, u32[]{:S(2)}) collective-permute-start(bf16[2,32,1024]{2,1,0:T(8,128)(2,1)S(1)} %get-tuple-element.848), channel_id=1, source_target_pairs={{0,8},{1,9},{2,10},{3,11},{4,12},{5,13},{6,14},{7,15}} | collective-permute-start | bytes 393224 | tf_op jit(solution)/shard_map/ppermute | solution.py:229
  49.5 8.0 %collective-permute-start.1 = (f32[2,32,1024]{2,1,0:T(8,128)S(1)}, f32[2,32,1024]{2,1,0:T(8,128)S(1)}, u32[]{:S(2)}, u32[]{:S(2)}) collective-permute-start(f32[2,32,1024]{2,1,0:T(8,128)S(1)} %get-tuple-element.849), channel_id=1, source_target_pairs={{8,0},{9,1},{10,2},{11,3},{12,4},{13,5},{14,6},{15,7}} | collective-permute-start | bytes 786440 | tf_op jit(solution)/shard_map/ppermute | solution.py:241
  50.8 12.3 %collective-permute-start.4 = (f32[2,32,1024]{2,1,0:T(8,128)S(1)}, f32[2,32,1024]{2,1,0:T(8,128)S(1)}, u32[]{:S(2)}, u32[]{:S(2)}) collective-permute-start(f32[2,32,1024]{2,1,0:T(8,128)S(1)} %broadcast_in_dim.17), channel_id=1, source_target_pairs={{8,0},{24,16},{40,32},{56,48},{72,64},{88,80},{104,96},{120,112},{... | collective-permute-start | bytes 786440 | tf_op jit(solution)/shard_map/ppermute | solution.py:217
  52.1 14.9 %collective-permute-start.3 = (f32[2,32,1024]{2,1,0:T(8,128)S(1)}, f32[2,32,1024]{2,1,0:T(8,128)S(1)}, u32[]{:S(2)}, u32[]{:S(2)}) collective-permute-start(f32[2,32,1024]{2,1,0:T(8,128)S(1)} %reshape.8), channel_id=1, source_target_pairs={{8,0},{24,16},{40,32},{56,48},{72,64},{88,80},{104,96},{120,112},{... | collective-permute-start | bytes 786440 | tf_op jit(solution)/shard_map/ppermute | solution.py:216
  53.4 9.7 %collective-permute-start.2 = (bf16[2,32,1024]{2,1,0:T(8,128)(2,1)S(1)}, bf16[2,32,1024]{2,1,0:T(8,128)(2,1)S(1)}, u32[]{:S(2)}, u32[]{:S(2)}) collective-permute-start(bf16[2,32,1024]{2,1,0:T(8,128)(2,1)S(1)} %get-tuple-element.850), channel_id=1, source_target_pairs={{8,16},{9,17},{10,18},{11,19},{12,20},{13,21},{14,22},{15,23}} | collective-permute-start | bytes 393224 | tf_op jit(solution)/shard_map/ppermute | solution.py:245
  67.7 0.7 collective-permute-start.7
  68.4 0.7 collective-permute-start.8
  69.1 0.7 collective-permute-start.9
  69.8 0.7 collective-permute-start.10
  71.2 0.7 collective-permute-start.23
  72.7 143.3 %all-gather.8.cloned.1.call-start = ((), (), s32[]{:S(2)}) async-start(), calls=%async_computation.4 | async-start | bytes 4718592 | tf_op jit(solution)/shard_map/all_gather | solution.py:260
  72.8 0.7 collective-permute-start.24
  74.3 0.7 collective-permute-start.12
  75.0 0.7 collective-permute-start.13
  75.7 0.7 collective-permute-start.14
  76.5 0.7 collective-permute-start.15
  77.2 0.7 collective-permute-start.16
  77.9 3.4 collective-permute-start.17
  78.5 3.5 collective-permute-start.21
  79.2 2.8 collective-permute-start.19
  79.9 2.1 collective-permute-start.22
  80.6 1.4 collective-permute-start.20
  81.3 0.7 collective-permute-start.18
  216.3 1.4 collective-permute-start.26
  217.0 0.7 collective-permute-start.25
  222.9 2.7 collective-permute-start.34
  223.6 2.0 collective-permute-start.35
  224.2 119.9 %collective-permute-start.36 = (f32[2,32,1024]{2,1,0:T(8,128)S(1)}, f32[2,32,1024]{2,1,0:T(8,128)S(1)}, u32[]{:S(2)}, u32[]{:S(2)}) collective-permute-start(f32[2,32,1024]{2,1,0:T(8,128)S(1)} %get-tuple-element.887), channel_id=1, source_target_pairs={{0,8},{32,40},{64,72},{96,104},{128,136},{160,168},{192,200},{224,... | collective-permute-start | bytes 786440 | tf_op jit(solution)/shard_map/ppermute | solution.py:302
  (12 other events, 8.5 us)
Sparse Core Ops, SparseCore 0:
  21.3 40.2 all-gather.3
  72.9 106.7 all-gather.5
  181.5 34.5 all-gather.7
